TPU v7x, 256 devices: a whole 4x4x8 slice. The times are simulated.
256 devices in a mesh: layer: 32 (over z, x), row: 2 (over core), col: 4 (over y).
Axes of the slice: x: 4, y: 4, z: 8, core: 2. Of those that a mesh axis runs over, the one named last changes fastest.
Arguments:
- left_factor: float32 [2048, 65536], P('row', ('layer', 'col')), may hold values from -6 to 6
- right_factor: float32 [65536, 4096], P(('layer', 'row'), 'col'), may hold values from -0.15625 to 0.15625
- left_pattern: int32 [32, 1024], P('row', ('layer', 'col')), may hold values 0 or 1
- right_pattern: int32 [1024, 64], P(('layer', 'row'), 'col'), may hold values 0 or 1
- product_pattern: int32 [32, 64], P('row', 'col'), may hold values 0 or 1
Outputs:
- product: float32 [2048, 4096], P(('layer', 'row'), 'col')
All inputs are finite; a program needn't handle non-finite values. No bound on the sum of `left_pattern` or of `right_pattern` or of `product_pattern` on one device may be relied on, other than what follows from the above.
Results may differ from a plain program's by a relative error of at most 0.000092.
Values sent between devices are 32-bit elements; how exact they have to be, the bound alone decides.
No kernel may reach another device: no remote copies, remote signals or barrier semaphores. Data moves between devices by JAX's collectives and lax.ppermute only.
A program may use at most 128 MiB of HBM per device.

v0:
```python
import jax
import jax.numpy as jnp
from jax import lax
from jax.sharding import PartitionSpec as P

BS = 64


def expand(pattern):
    return jnp.repeat(jnp.repeat(pattern.astype(jnp.float32), BS, axis=0), BS, axis=1)


def body(left_factor, right_factor, left_pattern, right_pattern, product_pattern):
    left = left_factor * expand(left_pattern)
    right = right_factor * expand(right_pattern)
    left_whole = lax.all_gather(left, "col", axis=1, tiled=True)
    partial_sum = jnp.dot(
        left_whole,
        lax.all_gather(right, "row", axis=0, tiled=True),
        preferred_element_type=jnp.float32,
        precision=lax.Precision.HIGHEST,
    )
    kept = partial_sum * expand(product_pattern)
    return lax.psum_scatter(kept, "layer", scatter_dimension=0, tiled=True)


def solution(mesh):
    return jax.shard_map(
        body,
        mesh=mesh,
        in_specs=(
            P("row", ("layer", "col")),
            P(("layer", "row"), "col"),
            P("row", ("layer", "col")),
            P(("layer", "row"), "col"),
            P("row", "col"),
        ),
        out_specs=P(("layer", "row"), "col"),
        check_vma=False,
    )
```

profile of v0, /device:TPU:8, one launch (start us, length us, event | category | flops | bytes accessed | tf_op | source)
XLA Modules:
  0.0 423.0 jit_solution(2757592346917892803)
XLA Ops:
  6.5 0.0 copy-start
  6.5 0.0 all-gather.5.cloned.1.call-start
  6.5 5.4 %copy.9 = f32[1024,1024]{0,1:T(8,128)} copy(f32[1024,1024]{1,0:T(8,128)} %param.6) | data formatting | bytes 8388608 | tf_op args[1]
  11.9 0.0 copy-done
  11.9 0.1 copy.8
  12.0 0.1 broadcast_in_dim.20
  12.1 0.1 reshape.20
  12.2 5.0 %bitcast_multiply_fusion = f32[1024,1024]{0,1:T(8,128)} fusion(f32[1024,1024]{0,1:T(8,128)} %copy.9, f32[1024,16]{0,1:T(8,128)S(1)} %reshape.20), kind=kLoop, calls=%fused_computation | loop fusion | flops 1048576 | bytes 8454144 | tf_op jit(solution)/shard_map/mul | solution.py:15
  17.2 0.0 copy-start.2
  17.2 0.0 all-gather.5.cloned.1.call-update
  17.2 0.0 all-gather.3.cloned.1.call-start
  17.3 1.9 copy.7
  19.2 0.0 copy-done.2
  19.2 0.0 copy-start.1
  19.3 0.1 broadcast_in_dim.18
  19.3 0.1 reshape.18
  19.4 1.5 bitcast_multiply_fusion.1
  21.0 0.0 all-gather.3.cloned.1.call-update
  21.0 0.0 reduce-scatter.2.cloned.1.call-start
  21.0 0.0 copy-done.1
  21.0 0.1 copy.10
  21.1 0.1 broadcast_in_dim.22
  21.2 0.1 reshape.22
  21.3 2.5 broadcast_in_dim.23
  23.8 5.4 %copy.11 = f32[1024,1024]{1,0:T(8,128)} copy(f32[1024,1024]{0,1:T(8,128)} %bitcast.13) | data formatting | bytes 8388608 | tf_op jit(solution)/shard_map/reshape | solution.py:10
  29.2 16.3 %all-gather.5.cloned.1.call-done = f32[2048,1024]{0,1:T(8,128)} async-done(((f32[1024,1024]{0,1:T(8,128)}), f32[2048,1024]{0,1:T(8,128)}) %all-gather.5.cloned.1.call-update) | async-done | bytes 8388624 | tf_op jit(solution)/shard_map/all_gather | solution.py:19
  45.5 88.7 %all-gather.3.cloned.1.call-done = f32[1024,2048]{0,1:T(8,128)} async-done(((f32[1024,512]{0,1:T(8,128)}), f32[1024,2048]{0,1:T(8,128)}) %all-gather.3.cloned.1.call-update) | async-done | bytes 8388624 | tf_op jit(solution)/shard_map/all_gather | solution.py:16
  134.2 57.5 %convolution_multiply_fusion = f32[1024,1024]{1,0:T(8,128)} fusion(f32[1024,1024]{1,0:T(8,128)} %copy.11, f32[1024,2048]{0,1:T(8,128)} %all-gather.3.cloned.1.call-done, f32[2048,1024]{0,1:T(8,128)} %all-gather.5.cloned.1.call-done), kind=kOutput, calls=%fused_computation.1 | convolution fusion | flops 25770852352 | bytes 25165824 | tf_op jit(solution)/shard_map/dot_general | solution.py:17
  191.7 0.0 reduce-scatter.2.cloned.1.call-update
  191.7 224.7 %reduce-scatter.2.cloned.1.call-done = f32[32,1024]{1,0:T(8,128)} async-done(((f32[1024,1024]{1,0:T(8,128)}), f32[32,1024]{1,0:T(8,128)}) %reduce-scatter.2.cloned.1.call-update) | async-done | bytes 131088 | tf_op jit(solution)/shard_map/reduce_scatter | solution.py:24
  (3 shorter events, 0.0 us)
Async XLA Ops:
  6.5 5.4 %copy-start = (s32[16,16]{1,0:T(8,128)S(1)}, s32[16,16]{1,0:T(8,128)}, u32[]{:S(2)}) copy-start(s32[16,16]{1,0:T(8,128)} %param.8) | copy-start | bytes 3076
  6.5 38.9 %all-gather.5.cloned.1.call-start = ((), (), s32[]{:S(2)}) async-start(), calls=%async_computation.2 | async-start | bytes 12582912 | tf_op jit(solution)/shard_map/all_gather | solution.py:19
  17.2 2.0 copy-start.2
  17.2 117.0 %all-gather.3.cloned.1.call-start = ((), (), s32[]{:S(2)}) async-start(), calls=%async_computation.1 | async-start | bytes 10485760 | tf_op jit(solution)/shard_map/all_gather | solution.py:16
  19.2 1.8 copy-start.1
  21.0 395.5 %reduce-scatter.2.cloned.1.call-start = ((), (), s32[]{:S(2)}) async-start(), calls=%async_computation.3 | async-start | bytes 4325376 | tf_op jit(solution)/shard_map/reduce_scatter | solution.py:24
Sparse Core Ops, SparseCore 0:
  17.4 28.0 all-gather.4
  47.3 86.8 all-gather.2
  191.8 224.5 reduce-scatter.1
where the time goes:
time: 423 us
  waiting for transfers between devices  330 us (78%)
  matrix products  57.5 us (14%)
  local copies, waits for them, and re-layouts  15.9 us (4%)
  between operations  13.2 us (3%)
  other arithmetic  6.55 us (2%)
    reduce_scatter x1, waiting for transfers between devices, body(): return lax.psum_scatter(kept, 'layer', scatter_dimension=0, tiled=True)  225 us
    all_gather x1, waiting for transfers between devices, body(): left_whole = lax.all_gather(left, 'col', axis=1, tiled=True)  88.7 us
    dot_general x1, matrix products, body(): jnp.dot(left_whole, lax.all_gather(right, 'row', axis=0, tiled=True), pre...  57.5 us
    all_gather x1, waiting for transfers between devices, body(): lax.all_gather(right, 'row', axis=0, tiled=True)  16.3 us
  transfers between devices with their start and end apart: 3, of which 3 were waited for; matrix products, arithmetic and copies ran while one was open for 3% of the time, Pallas kernels for 0%

commit v1 on v0

--- a/solution.py
+++ b/solution.py
@@ -16,7 +16,9 @@
     left_whole = lax.all_gather(left, "col", axis=1, tiled=True)
     partial_sum = jnp.dot(
         left_whole,
-        lax.all_gather(right, "row", axis=0, tiled=True),
+        jnp.concatenate(
+            lax.all_to_all(jnp.stack([right] * lax.axis_size("row")), "row", 0, 0), axis=0
+        ),
         preferred_element_type=jnp.float32,
         precision=lax.Precision.HIGHEST,
     )

time: 423 us -> 363 us (0.86)
  waiting for transfers between devices: 330 us -> 276 us
  matrix products: 57.5 us -> 31.9 us
  local copies, waits for them, and re-layouts: 15.9 us -> 24.6 us
  starting transfers between devices: 0.09 us -> 7.71 us
    all_gather x1, waiting for transfers between devices: 88.7 us -> 51.4 us  [body(): left_whole = lax.all_gather(left, 'col', axis=1, tiled=True)]
    dot_general x1, matrix products: 57.5 us -> 31.9 us  [body(): jnp.dot(left_whole, jnp.concatenate(lax.all_to_all(jnp.stack([right] * la...]
    all_gather x1 -> x0, waiting for transfers between devices: 16.3 us -> none  [body(): lax.all_gather(right, 'row', axis=0, tiled=True)]
    all_to_all x0 -> x1, local copies, waits for them, and re-layouts: none -> 8.75 us  [body(): lax.all_to_all(jnp.stack([right] * lax.axis_size('row')), 'row', 0, 0)]
    all_to_all x0 -> x1, starting transfers between devices: none -> 7.67 us  [body(): lax.all_to_all(jnp.stack([right] * lax.axis_size('row')), 'row', 0, 0)]
    another operation x0 -> x1, other arithmetic: none -> 4.29 us  [body(): jnp.stack([right] * lax.axis_size('row'))]
  transfers between devices with their start and end apart: 3 -> 3, of which waited for: 3 -> 2; matrix products, arithmetic and copies ran while one was open for 3% -> 8% of each run, Pallas kernels for 0% -> 0%
where the time goes in v1:
time: 363 us; the launch traced here: 362 us
  waiting for transfers between devices  276 us (76%)
  matrix products  31.9 us (9%)
  local copies, waits for them, and re-layouts  24.6 us (7%)
  between operations  13.5 us (4%)
  other arithmetic  8.5 us (2%)
  starting transfers between devices  7.71 us (2%)
    reduce_scatter x1, waiting for transfers between devices, body(): return lax.psum_scatter(kept, 'layer', scatter_dimension=0, tiled=True)  225 us
    all_gather x1, waiting for transfers between devices, body(): left_whole = lax.all_gather(left, 'col', axis=1, tiled=True)  51.4 us
    dot_general x1, matrix products, body(): jnp.dot(left_whole, jnp.concatenate(lax.all_to_all(jnp.stack([right] * la...  31.9 us
    all_to_all x1, local copies, waits for them, and re-layouts, body(): lax.all_to_all(jnp.stack([right] * lax.axis_size('row')), 'row', 0, 0)  8.75 us
    all_to_all x1, starting transfers between devices, body(): lax.all_to_all(jnp.stack([right] * lax.axis_size('row')), 'row', 0, 0)  7.67 us
    unnamed x8, local copies, waits for them, and re-layouts  7.32 us
  transfers between devices with their start and end apart: 3, of which 2 were waited for; matrix products, arithmetic and copies ran while one was open for 8% of the time, Pallas kernels for 0%

profile of v1, /device:TPU:8, one launch (start us, length us, event | category | flops | bytes accessed | tf_op | source)
XLA Modules:
  0.0 362.3 jit_solution(7018360422796637665)
XLA Ops:
  6.5 0.0 copy-start.2
  6.5 0.0 all-gather.2.cloned.1.call-start
  6.5 1.9 copy.12
  8.5 0.0 copy-done.2
  8.5 0.1 broadcast_in_dim.18
  8.6 0.1 reshape.21
  8.7 1.5 bitcast_multiply_fusion.1
  10.2 0.0 all-gather.2.cloned.1.call-update
  10.2 0.0 copy-start
  10.2 5.4 %copy.14 = f32[1024,1024]{0,1:T(8,128)} copy(f32[1024,1024]{1,0:T(8,128)} %param.6) | data formatting | bytes 8388608 | tf_op args[1]
  15.6 0.0 copy-done
  15.6 0.1 copy.13
  15.7 0.1 broadcast_in_dim.20
  15.8 0.1 reshape.23
  15.9 2.7 bitcast_multiply_fusion
  18.6 4.3 %pad_maximum_fusion = f32[2,1024,1024]{1,2,0:T(8,128)} fusion(f32[1,1024,1024]{1,2,0:T(8,128)S(1)} %bitcast.15), kind=kLoop, calls=%fused_computation | loop fusion | flops 2097152 | bytes 12582912 | tf_op jit(solution)/shard_map/stack | solution.py:20
  22.9 0.0 copy-start.1
  22.9 7.7 %all-to-all-start = ((f32[2,1024,1024]{1,2,0:T(8,128)}), f32[2,1024,1024]{1,2,0:T(8,128)}, u32[]{:S(2)}, u32[]{:S(2)}) async-start(f32[2,1024,1024]{1,2,0:T(8,128)} %pad_maximum_fusion), calls=%async_computation | async-start | bytes 16777216 | tf_op jit(solution)/shard_map/all_to_all | solution.py:20
  30.5 0.0 reduce-scatter.2.cloned.1.call-start
  30.6 0.0 copy-done.1
  30.6 0.1 copy.16
  30.7 0.1 broadcast_in_dim.22
  30.8 0.1 reshape.26
  30.9 2.5 broadcast_in_dim.23
  33.3 5.4 %copy.17 = f32[1024,1024]{1,0:T(8,128)} copy(f32[1024,1024]{0,1:T(8,128)} %bitcast.16) | data formatting | bytes 8388608 | tf_op jit(solution)/shard_map/reshape | solution.py:10
  38.7 0.0 all-to-all-done
  38.7 8.7 %copy.15 = f32[2,1024,1024]{2,1,0:T(8,128)} copy(f32[2,1024,1024]{1,2,0:T(8,128)} %all-to-all-done) | data formatting | bytes 16777216 | tf_op jit(solution)/shard_map/all_to_all | solution.py:20
  47.5 51.4 %all-gather.2.cloned.1.call-done = f32[1024,2048]{0,1:T(8,128)} async-done(((f32[1024,512]{0,1:T(8,128)}), f32[1024,2048]{0,1:T(8,128)}) %all-gather.2.cloned.1.call-update) | async-done | bytes 8388624 | tf_op jit(solution)/shard_map/all_gather | solution.py:16
  98.9 31.9 %convolution_multiply_fusion = f32[1024,1024]{1,0:T(8,128)} fusion(f32[1024,1024]{1,0:T(8,128)} %copy.17, f32[1024,2048]{0,1:T(8,128)} %all-gather.2.cloned.1.call-done, f32[2048,1024]{1,0:T(8,128)} %bitcast.17), kind=kOutput, calls=%fused_computation.2 | convolution fusion | flops 25770852352 | bytes 25165824 | tf_op jit(solution)/shard_map/dot_general | solution.py:17
  130.8 0.0 reduce-scatter.2.cloned.1.call-update
  130.8 224.6 %reduce-scatter.2.cloned.1.call-done = f32[32,1024]{1,0:T(8,128)} async-done(((f32[1024,1024]{1,0:T(8,128)}), f32[32,1024]{1,0:T(8,128)}) %reduce-scatter.2.cloned.1.call-update) | async-done | bytes 131088 | tf_op jit(solution)/shard_map/reduce_scatter | solution.py:26
  (3 shorter events, 0.0 us)
Async XLA Ops:
  6.5 1.9 copy-start.2
  6.5 92.3 %all-gather.2.cloned.1.call-start = ((), (), s32[]{:S(2)}) async-start(), calls=%async_computation.2 | async-start | bytes 10485760 | tf_op jit(solution)/shard_map/all_gather | solution.py:16
  10.2 5.4 %copy-start = (s32[16,16]{1,0:T(8,128)S(1)}, s32[16,16]{1,0:T(8,128)}, u32[]{:S(2)}) copy-start(s32[16,16]{1,0:T(8,128)} %param.8) | copy-start | bytes 3076
  22.9 7.7 %copy-start.1 = (s32[16,16]{1,0:T(8,128)S(1)}, s32[16,16]{1,0:T(8,128)}, u32[]{:S(2)}) copy-start(s32[16,16]{1,0:T(8,128)} %param.9) | copy-start | bytes 3076
  22.9 15.9 %all-to-all-start = ((f32[2,1024,1024]{1,2,0:T(8,128)}), f32[2,1024,1024]{1,2,0:T(8,128)}, u32[]{:S(2)}, u32[]{:S(2)}) async-start(f32[2,1024,1024]{1,2,0:T(8,128)} %pad_maximum_fusion), calls=%async_computation | async-start | bytes 16777216 | tf_op jit(solution)/shard_map/all_to_all | solution.py:20
  30.5 324.9 %reduce-scatter.2.cloned.1.call-start = ((), (), s32[]{:S(2)}) async-start(), calls=%async_computation.3 | async-start | bytes 4325376 | tf_op jit(solution)/shard_map/reduce_scatter | solution.py:26
Sparse Core Ops, SparseCore 0:
  10.3 88.4 all-gather.1
  131.0 224.4 reduce-scatter.1
